TPU v7x, 512 devices: a whole 4x8x8 slice. The times are simulated.
512 devices in a mesh: req: 64 (over x, z, core), ch: 8 (over y).
Axes of the slice: x: 4, y: 8, z: 8, core: 2. Of those that a mesh axis runs over, the one named last changes fastest.
Arguments:
- tokens: bfloat16 [128, 4096], P('req', 'ch'), may hold values from -80 to 80
- attn_gain: float32 [4096], P('ch'), may hold values from 0.1 to 1.9
- w_query: bfloat16 [4096, 4096], P('ch', 'req'), may hold values from -0.09375 to 0.09375
- w_keyval: bfloat16 [4096, 512], P('ch', 'req'), may hold values from -0.09375 to 0.09375
- cache: bfloat16 [2, 128, 256, 2048], P(None, 'req', 'ch'), may hold values from -70 to 70
- lengths: int32 [128], P('req'), may hold values from 1 to 2047, as said below
- write_pos: int32 [128], P('req'), may hold values from 0 to 2047
- w_out: bfloat16 [4096, 4096], P('ch', 'req'), may hold values from -0.09375 to 0.09375
- mlp_gain: float32 [4096], P('ch'), may hold values from 0.1 to 1.9
- w_gate_up: bfloat16 [4096, 24576], P('ch', 'req'), may hold values from -0.09375 to 0.09375
- w_down: bfloat16 [12288, 4096], P('req', 'ch'), may hold values from -0.0546875 to 0.0546875
Outputs:
- layer_out: bfloat16 [128, 4096], P('req', 'ch')
- kv_new: bfloat16 [128, 512], P('req', 'ch')
Inputs may be any that keep to these rules, and one draw needn't show every extreme that they name: lengths[b] earlier tokens of request b are in the cache; the largest equals 2047 in every draw. The new token of request b goes to slot write_pos[b]; its earlier tokens fill the slots before it, going back cyclically.
All inputs are finite; a program needn't handle non-finite values.
Results may differ from a plain program's by a relative error of at most 0.0064.
Values may be sent and summed in bfloat16 or wider, within the bound.
No kernel may reach another device: no remote copies, remote signals or barrier semaphores. Data moves between devices by JAX's collectives and lax.ppermute only.
A program may use at most 64 MiB of HBM per device.

v0:
```python
import math
import jax
import jax.numpy as jnp
from jax import lax
from jax.sharding import PartitionSpec as P

D = 4096
H = 16
HD = 256
EPSILON = 1e-06


def rms_norm(values, gain):
    wide = values.astype(jnp.float32)
    squares = jnp.sum(wide * wide, axis=1)
    summed = lax.psum(squares, "ch")
    meansq = summed / D
    return (wide * lax.rsqrt(meansq + EPSILON)[:, None] * gain[None, :]).astype(jnp.bfloat16)


def body(
    tokens,
    attn_gain,
    w_query,
    w_keyval,
    cache,
    lengths,
    write_pos,
    w_out,
    mlp_gain,
    w_gate_up,
    w_down,
):
    rows = tokens.shape[0]
    chan = cache.shape[2]
    window = cache.shape[3]
    factor = 1.0 / math.sqrt(HD)
    normed = rms_norm(tokens, attn_gain)
    joined = jnp.concatenate([w_query, w_keyval], axis=1)
    head_parts = jnp.dot(
        lax.all_gather(normed, "req", axis=0, tiled=True),
        joined,
        preferred_element_type=jnp.float32,
    )
    query_cols = w_query.shape[1]
    query_part, keyval_part = (
        lax.all_to_all(head_parts[:, :query_cols], "req", split_axis=0, concat_axis=1, tiled=True),
        lax.all_to_all(head_parts[:, query_cols:], "req", split_axis=0, concat_axis=1, tiled=True),
    )
    query_sum, keyval_sum = (
        lax.psum_scatter(query_part, "ch", scatter_dimension=1, tiled=True),
        lax.psum_scatter(keyval_part, "ch", scatter_dimension=1, tiled=True),
    )
    queries = query_sum.astype(jnp.bfloat16).reshape(rows, H, chan)
    keyval_new = keyval_sum.astype(jnp.bfloat16)
    key_new = keyval_new[:, :chan]
    value_new = keyval_new[:, chan:]
    keys = cache[0]
    values_cache = cache[1]
    own_part = jnp.sum(
        queries.astype(jnp.float32) * key_new.astype(jnp.float32)[:, None, :], axis=-1
    )
    score_part = jnp.einsum("bhe,bew->bhw", queries, keys, preferred_element_type=jnp.float32)
    summed, own_sum = lax.psum((score_part, own_part), "ch")
    slot_index = jnp.arange(window, dtype=jnp.int32)
    offset = (write_pos[:, None] - 1 - slot_index[None, :]) % window
    usable = offset < lengths[:, None]
    scores = jnp.where(usable[:, None, :], summed * factor, -jnp.inf)
    own_score = own_sum * factor
    top = jnp.maximum(jnp.max(scores, axis=-1), own_score)
    weights = jnp.exp(scores - top[..., None])
    own_weight = jnp.exp(own_score - top)
    total = jnp.sum(weights, axis=-1) + own_weight
    weights_low = weights.astype(jnp.bfloat16)
    numer = jnp.einsum(
        "bhw,bew->bhe", weights_low, values_cache, preferred_element_type=jnp.float32
    )
    numer = (
        numer
        + own_weight.astype(jnp.bfloat16).astype(jnp.float32)[..., None]
        * value_new.astype(jnp.float32)[:, None, :]
    )
    attn_local = (numer / total[..., None]).astype(jnp.bfloat16).reshape(rows, H * chan)
    out_parts = jnp.dot(
        lax.all_gather(attn_local, "req", axis=0, tiled=True),
        w_out,
        preferred_element_type=jnp.float32,
    )
    out_part = lax.all_to_all(out_parts, "req", split_axis=0, concat_axis=1, tiled=True)
    out_sum = lax.psum_scatter(out_part, "ch", scatter_dimension=1, tiled=True)
    first = (tokens.astype(jnp.float32) + out_sum).astype(jnp.bfloat16)
    normed_two = rms_norm(first, mlp_gain)
    hidden_cols = w_gate_up.shape[1] // 2
    ffn_parts = jnp.dot(
        lax.all_gather(normed_two, "req", axis=0, tiled=True),
        w_gate_up,
        preferred_element_type=jnp.float32,
    )
    ffn_total = lax.psum(ffn_parts, "ch")
    hidden = (
        jax.nn.gelu(ffn_total[:, :hidden_cols], approximate=True) * ffn_total[:, hidden_cols:]
    ).astype(jnp.bfloat16)
    down_sum = lax.psum_scatter(
        jnp.dot(hidden, w_down, preferred_element_type=jnp.float32),
        "req",
        scatter_dimension=0,
        tiled=True,
    )
    layer_out = (first.astype(jnp.float32) + down_sum).astype(jnp.bfloat16)
    return (layer_out, keyval_new)


def solution(mesh):
    placed = (
        P("req", "ch"),
        P("ch"),
        P("ch", "req"),
        P("ch", "req"),
        P(None, "req", "ch", None),
        P("req"),
        P("req"),
        P("ch", "req"),
        P("ch"),
        P("ch", "req"),
        P("req", "ch"),
    )
    return jax.shard_map(
        body,
        mesh=mesh,
        in_specs=placed,
        out_specs=(P("req", "ch"), P("req", "ch")),
        check_vma=False,
    )
```

profile of v0, /device:TPU:1, one launch (start us, length us, event | category | flops | bytes accessed | tf_op | source)
XLA Modules:
  0.0 728.1 jit_solution(11447148937282177522)
XLA Ops:
  8.0 14.7 %psum.35 = f32[2]{0:T(128)S(1)} all-reduce(f32[2]{0:T(128)S(1)} %fusion.36), channel_id=1, replica_groups=mesh['req'=64,'ch'=8] {'ch'}, use_global_device_ids=true, to_apply=%region_1.0 | all-reduce | flops 2 | bytes 16 | tf_op jit(solution)/shard_map/psum | solution.py:16
  23.5 60.2 %all-gather = bf16[64,2,512]{2,1,0:T(2,128)(2,1)S(1)} all-gather(bf16[1,2,512]{2,1,0:T(2,128)(2,1)S(1)} %fusion.45), channel_id=1, replica_groups=mesh['req'=64,'ch'=8] {'req'}, dimensions={0}, use_global_device_ids=true | all-gather | bytes 133120 | tf_op jit(solution)/shard_map/all_gather | solution.py:41
  85.5 5.6 all-to-all-start.1
  91.9 8.9 %all-to-all-done.1 = f32[64,2,8]{2,1,0:T(2,128)S(1)} async-done(((f32[64,2,8]{2,1,0:T(2,128)}), f32[64,2,8]{2,1,0:T(2,128)S(1)}, u32[]{:S(2)}, u32[]{:S(2)}) %all-to-all-start.1) | async-done | bytes 4128 | tf_op jit(solution)/shard_map/all_to_all | solution.py:48
  100.8 4.4 all-to-all-start
  105.2 1.2 copy.40
  107.2 7.5 %all-to-all-done = f32[64,1,128]{2,1,0:T(1,128)S(1)} async-done(((f32[64,1,128]{2,1,0:T(1,128)}), f32[64,1,128]{2,1,0:T(1,128)S(1)}, u32[]{:S(2)}, u32[]{:S(2)}) %all-to-all-start) | async-done | bytes 32800 | tf_op jit(solution)/shard_map/all_to_all | solution.py:47
  116.0 2.0 copy.39
  118.2 23.1 %reduce-scatter.12.cloned.1.call-done = f32[64,2]{1,0:T(8,128)} async-done(((f32[512,2]{1,0:T(8,128)}), f32[64,2]{1,0:T(8,128)}) %reduce-scatter.12.cloned.1.call-update) | async-done | bytes 528
  142.2 47.1 %reduce-scatter.10.cloned.1.call-done = f32[512,2]{1,0:T(8,128)} async-done(((f32[4096,2]{1,0:T(8,128)}), f32[512,2]{1,0:T(8,128)}) %reduce-scatter.10.cloned.1.call-update) | async-done | bytes 4112
  191.6 11.9 %psum.37 = f32[2,16]{1,0:T(2,128)S(1)} all-reduce(f32[2,16]{1,0:T(2,128)S(1)} %multiply_reduce_fusion), channel_id=1, replica_groups=mesh['req'=64,'ch'=8] {'ch'}, use_global_device_ids=true, to_apply=%region_7.8 | all-reduce | flops 32 | bytes 256 | tf_op jit(solution)/shard_map/psum | solution.py:64
  203.5 64.4 %all-reduce.5.cloned.1.call-done = f32[2,16,2048]{2,1,0:T(8,128)} async-done(((f32[2,16,2048]{2,1,0:T(8,128)}), f32[2,16,2048]{2,1,0:T(8,128)}) %all-reduce.5.cloned.1.call-update) | async-done | bytes 262160 | tf_op jit(solution)/shard_map/psum | solution.py:64
  270.1 1.2 fusion.1
  271.4 57.0 %all-gather.1 = bf16[64,2,512]{2,1,0:T(2,128)(2,1)S(1)} all-gather(bf16[1,2,512]{2,1,0:T(2,128)(2,1)S(1)} %reshape.73), channel_id=1, replica_groups=mesh['req'=64,'ch'=8] {'req'}, dimensions={0}, use_global_device_ids=true | all-gather | bytes 133120 | tf_op jit(solution)/shard_map/all_gather | solution.py:85
  328.8 16.1 %all_to_all.57 = f32[64,1,128]{2,1,0:T(1,128)S(1)} all-to-all(f32[64,1,128]{2,1,0:T(1,128)S(1)} %reshape.87), channel_id=1, replica_groups=mesh['req'=64,'ch'=8] {'req'}, dimensions={0} | all-to-all | bytes 65536 | tf_op jit(solution)/shard_map/all_to_all | solution.py:89
  345.8 2.0 copy.41
  347.9 32.4 %reduce-scatter.14.cloned.1.call-done = f32[512,2]{1,0:T(8,128)} async-done(((f32[4096,2]{1,0:T(8,128)}), f32[512,2]{1,0:T(8,128)}) %reduce-scatter.14.cloned.1.call-update) | async-done | bytes 4112
  381.5 12.0 %psum.38 = f32[2]{0:T(128)S(1)} all-reduce(f32[2]{0:T(128)S(1)} %get-tuple-element.2), channel_id=1, replica_groups=mesh['req'=64,'ch'=8] {'ch'}, use_global_device_ids=true, to_apply=%region_11.12 | all-reduce | flops 2 | bytes 16 | tf_op jit(solution)/shard_map/psum | solution.py:16
  393.6 59.6 %all-gather.2 = bf16[64,2,512]{2,1,0:T(2,128)(2,1)S(1)} all-gather(bf16[1,2,512]{2,1,0:T(2,128)(2,1)S(1)} %fusion.44), channel_id=1, replica_groups=mesh['req'=64,'ch'=8] {'req'}, dimensions={0}, use_global_device_ids=true | all-gather | bytes 133120 | tf_op jit(solution)/shard_map/all_gather | solution.py:95
  454.2 69.2 %all-reduce.7.cloned.1.call-done = f32[128,384]{1,0:T(8,128)} async-done(((f32[128,384]{1,0:T(8,128)}), f32[128,384]{1,0:T(8,128)}) %all-reduce.7.cloned.1.call-update) | async-done | bytes 196624 | tf_op jit(solution)/shard_map/psum | solution.py:99
  523.4 1.9 fusion.28
  525.3 1.3 dynamic-slice
  527.3 192.7 %all-reduce.9.cloned.1.call-done = f32[128,512]{1,0:T(8,128)} async-done(((f32[128,512]{1,0:T(8,128)}), f32[128,512]{1,0:T(8,128)}) %all-reduce.9.cloned.1.call-update) | async-done | bytes 262160
  720.0 1.3 fusion.43
  (65 shorter events, 15.5 us)
Async XLA Ops:
  7.2 446.1 %copy-start = (bf16[512,384]{1,0:T(8,128)(2,1)S(1)}, bf16[512,384]{1,0:T(8,128)(2,1)}, u32[]{:S(2)}) copy-start(bf16[512,384]{1,0:T(8,128)(2,1)} %param.20) | copy-start | bytes 1179652
  85.5 15.3 %all-to-all-start.1 = ((f32[64,2,8]{2,1,0:T(2,128)}), f32[64,2,8]{2,1,0:T(2,128)S(1)}, u32[]{:S(2)}, u32[]{:S(2)}) async-start(f32[64,2,8]{2,1,0:T(2,128)} %bitcast.4), calls=%async_computation.1 | async-start | bytes 131072 | tf_op jit(solution)/shard_map/all_to_all | solution.py:48
  100.8 13.8 %all-to-all-start = ((f32[64,1,128]{2,1,0:T(1,128)}), f32[64,1,128]{2,1,0:T(1,128)S(1)}, u32[]{:S(2)}, u32[]{:S(2)}) async-start(f32[64,1,128]{2,1,0:T(1,128)} %reshape.85), calls=%async_computation | async-start | bytes 65536 | tf_op jit(solution)/shard_map/all_to_all | solution.py:47
  105.2 36.1 %reduce-scatter.12.cloned.1.call-start = ((), (), s32[]{:S(2)}) async-start(), calls=%async_computation.9 | async-start | bytes 294912
  106.4 82.9 %reduce-scatter.10.cloned.1.call-start = ((), (), s32[]{:S(2)}) async-start(), calls=%async_computation.8 | async-start | bytes 2359296
  116.0 2.2 copy-start.7
  116.0 74.5 %copy-start.2 = (bf16[2,2,32,2048]{3,2,1,0:T(8,128)(2,1)S(1)}, bf16[2,2,32,2048]{3,2,1,0:T(8,128)(2,1)}, u32[]{:S(2)}) copy-start(bf16[2,2,32,2048]{3,2,1,0:T(8,128)(2,1)} %param.15) | copy-start | bytes 1572868
  118.0 210.5 %copy-start.3 = (bf16[512,64]{0,1:T(8,128)(2,1)S(1)}, bf16[512,64]{0,1:T(8,128)(2,1)}, u32[]{:S(2)}) copy-start(bf16[512,64]{0,1:T(8,128)(2,1)} %param.18) | copy-start | bytes 196612
  118.1 149.8 %all-reduce.5.cloned.1.call-start = ((), (), s32[]{:S(2)}) async-start(), calls=%async_computation.6 | async-start | bytes 524288 | tf_op jit(solution)/shard_map/psum | solution.py:64
  142.2 205.6 %copy-start.5 = (bf16[2,64]{1,0:T(2,128)(2,1)}, bf16[2,64]{1,0:T(2,128)(2,1)S(1)}, u32[]{:S(2)}) copy-start(bf16[2,64]{1,0:T(2,128)(2,1)S(1)} %copy.36) | copy-start | bytes 772
  191.4 188.9 %reduce-scatter.14.cloned.1.call-start = ((), (), s32[]{:S(2)}) async-start(), calls=%async_computation.10 | async-start | bytes 2359296
  345.7 35.6 %copy-start.4 = (bf16[2,512]{1,0:T(2,128)(2,1)S(1)}, bf16[2,512]{1,0:T(2,128)(2,1)}, u32[]{:S(2)}) copy-start(bf16[2,512]{1,0:T(2,128)(2,1)} %param.11) | copy-start | bytes 6148
  345.8 47.8 %copy-start.6 = (f32[512]{0:T(512)S(1)}, f32[512]{0:T(512)}, u32[]{:S(2)}) copy-start(f32[512]{0:T(512)} %param.19) | copy-start | bytes 6148
  347.8 175.6 %copy-start.1 = (bf16[192,512]{1,0:T(8,128)(2,1)S(1)}, bf16[192,512]{1,0:T(8,128)(2,1)}, u32[]{:S(2)}) copy-start(bf16[192,512]{1,0:T(8,128)(2,1)} %param.21) | copy-start | bytes 589828
  347.8 175.6 %all-reduce.7.cloned.1.call-start = ((), (), s32[]{:S(2)}) async-start(), calls=%async_computation.7 | async-start | bytes 393216 | tf_op jit(solution)/shard_map/psum | solution.py:99
  454.2 265.8 %all-reduce.9.cloned.1.call-start = ((), (), s32[]{:S(2)}) async-start(), calls=%async_computation.11 | async-start | bytes 524288
Sparse Core Ops, SparseCore 0:
  108.8 32.4 reduce-scatter.11
  144.2 45.0 reduce-scatter.9
  191.6 76.2 all-reduce.4
  348.0 32.2 reduce-scatter.13
  454.3 69.0 all-reduce.6
  526.7 193.2 all-reduce.8
where the time goes:
time: 729 us; the launch traced here: 728 us
  waiting for transfers between devices  446 us (61%)
  blocking collectives  231 us (32%)
  between operations  15 us (2%)
  local copies, waits for them, and re-layouts  12.2 us (2%)
  starting transfers between devices  10.2 us (1%)
  other arithmetic  7.74 us (1%)
    unnamed x10, waiting for transfers between devices  295 us
    psum x1, waiting for transfers between devices, body(): ffn_total = lax.psum(ffn_parts, 'ch')  69.2 us
    psum x1, waiting for transfers between devices, body(): summed, own_sum = lax.psum((score_part, own_part), 'ch')  64.4 us
    all_gather x1, blocking collectives, body(): lax.all_gather(normed, 'req', axis=0, tiled=True)  60.2 us
    all_gather x1, blocking collectives, body(): lax.all_gather(normed_two, 'req', axis=0, tiled=True)  59.6 us
    all_gather x1, blocking collectives, body(): lax.all_gather(attn_local, 'req', axis=0, tiled=True)  57 us
    psum x2, blocking collectives, rms_norm(): summed = lax.psum(squares, 'ch')  26.7 us
    all_to_all x1, blocking collectives, body(): lax.all_to_all(out_parts, 'req', split_axis=0, concat_axis=1, tiled=True)  16.1 us
  transfers between devices with their start and end apart: 8, of which 8 were waited for; matrix products, arithmetic and copies ran while one was open for 1% of the time, Pallas kernels for 0%

commit v1 on v0

--- a/solution.py
+++ b/solution.py
@@ -8,6 +8,11 @@
 H = 16
 HD = 256
 EPSILON = 1e-06
+
+
+def gather_from_all(shard, axis, dim):
+    copies = jnp.concatenate([shard] * lax.axis_size(axis), axis=dim)
+    return lax.all_to_all(copies, axis, dim, dim, tiled=True)
 
 
 def rms_norm(values, gain):
@@ -38,9 +43,7 @@
     normed = rms_norm(tokens, attn_gain)
     joined = jnp.concatenate([w_query, w_keyval], axis=1)
     head_parts = jnp.dot(
-        lax.all_gather(normed, "req", axis=0, tiled=True),
-        joined,
-        preferred_element_type=jnp.float32,
+        gather_from_all(normed, "req", 0), joined, preferred_element_type=jnp.float32
     )
     query_cols = w_query.shape[1]
     query_part, keyval_part = (

time: 729 us -> 696 us (0.955)
  blocking collectives: 231 us -> 199 us
    all_gather x1 -> x0, blocking collectives: 60.2 us -> none  [body(): lax.all_gather(normed, 'req', axis=0, tiled=True)]
    all_to_all x0 -> x1, blocking collectives: none -> 27.9 us  [gather_from_all(): return lax.all_to_all(copies, axis, dim, dim, tiled=True)]
where the time goes in v1:
time: 696 us
  waiting for transfers between devices  446 us (64%)
  blocking collectives  199 us (29%)
  between operations  15 us (2%)
  local copies, waits for them, and re-layouts  12.8 us (2%)
  starting transfers between devices  9.49 us (1%)
  other arithmetic  7.09 us (1%)
    unnamed x10, waiting for transfers between devices  296 us
    psum x1, waiting for transfers between devices, body(): ffn_total = lax.psum(ffn_parts, 'ch')  68.9 us
    psum x1, waiting for transfers between devices, body(): summed, own_sum = lax.psum((score_part, own_part), 'ch')  64.5 us
    all_gather x1, blocking collectives, body(): lax.all_gather(normed_two, 'req', axis=0, tiled=True)  59.6 us
    all_gather x1, blocking collectives, body(): lax.all_gather(attn_local, 'req', axis=0, tiled=True)  57 us
    all_to_all x1, blocking collectives, gather_from_all(): return lax.all_to_all(copies, axis, dim, dim, tiled=True)  27.9 us
    psum x2, blocking collectives, rms_norm(): summed = lax.psum(squares, 'ch')  26.7 us
    all_to_all x1, blocking collectives, body(): lax.all_to_all(out_parts, 'req', split_axis=0, concat_axis=1, tiled=True)  16.1 us
  transfers between devices with their start and end apart: 8, of which 8 were waited for; matrix products, arithmetic and copies ran while one was open for 1% of the time, Pallas kernels for 0%

profile of v1, /device:TPU:1, one launch (start us, length us, event | category | flops | bytes accessed | tf_op | source)
XLA Modules:
  0.0 695.5 jit_solution(11802664696209583861)
XLA Ops:
  8.0 14.7 %psum.35 = f32[2]{0:T(128)S(1)} all-reduce(f32[2]{0:T(128)S(1)} %fusion.36), channel_id=1, replica_groups=mesh['req'=64,'ch'=8] {'ch'}, use_global_device_ids=true, to_apply=%region_1.0 | all-reduce | flops 2 | bytes 16 | tf_op jit(solution)/shard_map/psum | solution.py:21
  24.1 27.9 %all_to_all.69 = bf16[64,2,512]{2,1,0:T(2,128)(2,1)S(1)} all-to-all(bf16[64,2,512]{2,1,0:T(2,128)(2,1)S(1)} %all_to_all.50), channel_id=1, replica_groups=mesh['req'=64,'ch'=8] {'req'}, dimensions={0} | all-to-all | bytes 262144 | tf_op jit(solution)/shard_map/all_to_all | solution.py:15
  53.8 4.9 all-to-all-start.2
  59.5 8.9 %all-to-all-done.2 = f32[64,2,8]{2,1,0:T(2,128)S(1)} async-done(((f32[64,2,8]{2,1,0:T(2,128)}), f32[64,2,8]{2,1,0:T(2,128)S(1)}, u32[]{:S(2)}, u32[]{:S(2)}) %all-to-all-start.2) | async-done | bytes 4128 | tf_op jit(solution)/shard_map/all_to_all | solution.py:51
  68.5 4.4 all-to-all-start.1
  72.9 1.2 copy.40
  74.2 8.1 %all-to-all-done.1 = f32[64,1,128]{2,1,0:T(1,128)S(1)} async-done(((f32[64,1,128]{2,1,0:T(1,128)}), f32[64,1,128]{2,1,0:T(1,128)S(1)}, u32[]{:S(2)}, u32[]{:S(2)}) %all-to-all-start.1) | async-done | bytes 32800 | tf_op jit(solution)/shard_map/all_to_all | solution.py:50
  83.7 2.0 copy.39
  85.9 23.1 %reduce-scatter.12.cloned.1.call-done = f32[64,2]{1,0:T(8,128)} async-done(((f32[512,2]{1,0:T(8,128)}), f32[64,2]{1,0:T(8,128)}) %reduce-scatter.12.cloned.1.call-update) | async-done | bytes 528
  109.8 47.1 %reduce-scatter.10.cloned.1.call-done = f32[512,2]{1,0:T(8,128)} async-done(((f32[4096,2]{1,0:T(8,128)}), f32[512,2]{1,0:T(8,128)}) %reduce-scatter.10.cloned.1.call-update) | async-done | bytes 4112
  159.2 11.8 %psum.37 = f32[2,16]{1,0:T(2,128)S(1)} all-reduce(f32[2,16]{1,0:T(2,128)S(1)} %multiply_reduce_fusion), channel_id=1, replica_groups=mesh['req'=64,'ch'=8] {'ch'}, use_global_device_ids=true, to_apply=%region_7.8 | all-reduce | flops 32 | bytes 256 | tf_op jit(solution)/shard_map/psum | solution.py:67
  171.1 64.5 %all-reduce.5.cloned.1.call-done = f32[2,16,2048]{2,1,0:T(8,128)} async-done(((f32[2,16,2048]{2,1,0:T(8,128)}), f32[2,16,2048]{2,1,0:T(8,128)}) %all-reduce.5.cloned.1.call-update) | async-done | bytes 262160 | tf_op jit(solution)/shard_map/psum | solution.py:67
  237.8 1.2 fusion.1
  239.1 57.0 %all-gather = bf16[64,2,512]{2,1,0:T(2,128)(2,1)S(1)} all-gather(bf16[1,2,512]{2,1,0:T(2,128)(2,1)S(1)} %reshape.73), channel_id=1, replica_groups=mesh['req'=64,'ch'=8] {'req'}, dimensions={0}, use_global_device_ids=true | all-gather | bytes 133120 | tf_op jit(solution)/shard_map/all_gather | solution.py:88
  296.4 16.1 %all_to_all.70 = f32[64,1,128]{2,1,0:T(1,128)S(1)} all-to-all(f32[64,1,128]{2,1,0:T(1,128)S(1)} %reshape.87), channel_id=1, replica_groups=mesh['req'=64,'ch'=8] {'req'}, dimensions={0} | all-to-all | bytes 65536 | tf_op jit(solution)/shard_map/all_to_all | solution.py:92
  313.4 2.0 copy.41
  315.5 32.4 %reduce-scatter.14.cloned.1.call-done = f32[512,2]{1,0:T(8,128)} async-done(((f32[4096,2]{1,0:T(8,128)}), f32[512,2]{1,0:T(8,128)}) %reduce-scatter.14.cloned.1.call-update) | async-done | bytes 4112
  349.2 12.0 %psum.38 = f32[2]{0:T(128)S(1)} all-reduce(f32[2]{0:T(128)S(1)} %get-tuple-element.2), channel_id=1, replica_groups=mesh['req'=64,'ch'=8] {'ch'}, use_global_device_ids=true, to_apply=%region_11.12 | all-reduce | flops 2 | bytes 16 | tf_op jit(solution)/shard_map/psum | solution.py:21
  361.2 59.6 %all-gather.1 = bf16[64,2,512]{2,1,0:T(2,128)(2,1)S(1)} all-gather(bf16[1,2,512]{2,1,0:T(2,128)(2,1)S(1)} %fusion.44), channel_id=1, replica_groups=mesh['req'=64,'ch'=8] {'req'}, dimensions={0}, use_global_device_ids=true | all-gather | bytes 133120 | tf_op jit(solution)/shard_map/all_gather | solution.py:98
  421.9 68.9 %all-reduce.7.cloned.1.call-done = f32[128,384]{1,0:T(8,128)} async-done(((f32[128,384]{1,0:T(8,128)}), f32[128,384]{1,0:T(8,128)}) %all-reduce.7.cloned.1.call-update) | async-done | bytes 196624 | tf_op jit(solution)/shard_map/psum | solution.py:102
  490.8 1.9 fusion.28
  492.7 1.3 dynamic-slice
  494.6 192.7 %all-reduce.9.cloned.1.call-done = f32[128,512]{1,0:T(8,128)} async-done(((f32[128,512]{1,0:T(8,128)}), f32[128,512]{1,0:T(8,128)}) %all-reduce.9.cloned.1.call-update) | async-done | bytes 262160
  687.4 1.3 fusion.43
  (69 shorter events, 15.4 us)
Async XLA Ops:
  7.2 413.7 %copy-start = (bf16[512,384]{1,0:T(8,128)(2,1)S(1)}, bf16[512,384]{1,0:T(8,128)(2,1)}, u32[]{:S(2)}) copy-start(bf16[512,384]{1,0:T(8,128)(2,1)} %param.20) | copy-start | bytes 1179652
  7.2 67.0 %copy-start.8 = (s32[2]{0:T(128)S(1)}, s32[2]{0:T(128)}, u32[]{:S(2)}) copy-start(s32[2]{0:T(128)} %param.17) | copy-start | bytes 28
  53.8 14.7 %all-to-all-start.2 = ((f32[64,2,8]{2,1,0:T(2,128)}), f32[64,2,8]{2,1,0:T(2,128)S(1)}, u32[]{:S(2)}, u32[]{:S(2)}) async-start(f32[64,2,8]{2,1,0:T(2,128)} %bitcast.3), calls=%async_computation.2 | async-start | bytes 131072 | tf_op jit(solution)/shard_map/all_to_all | solution.py:51
  68.5 13.8 %all-to-all-start.1 = ((f32[64,1,128]{2,1,0:T(1,128)}), f32[64,1,128]{2,1,0:T(1,128)S(1)}, u32[]{:S(2)}, u32[]{:S(2)}) async-start(f32[64,1,128]{2,1,0:T(1,128)} %reshape.85), calls=%async_computation.1 | async-start | bytes 65536 | tf_op jit(solution)/shard_map/all_to_all | solution.py:50
  72.9 36.1 %reduce-scatter.12.cloned.1.call-start = ((), (), s32[]{:S(2)}) async-start(), calls=%async_computation.10 | async-start | bytes 294912
  74.1 82.9 %reduce-scatter.10.cloned.1.call-start = ((), (), s32[]{:S(2)}) async-start(), calls=%async_computation.9 | async-start | bytes 2359296
  83.6 2.1 copy-start.7
  83.6 74.5 %copy-start.2 = (bf16[2,2,32,2048]{3,2,1,0:T(8,128)(2,1)S(1)}, bf16[2,2,32,2048]{3,2,1,0:T(8,128)(2,1)}, u32[]{:S(2)}) copy-start(bf16[2,2,32,2048]{3,2,1,0:T(8,128)(2,1)} %param.15) | copy-start | bytes 1572868
  85.7 210.4 %copy-start.3 = (bf16[512,64]{0,1:T(8,128)(2,1)S(1)}, bf16[512,64]{0,1:T(8,128)(2,1)}, u32[]{:S(2)}) copy-start(bf16[512,64]{0,1:T(8,128)(2,1)} %param.18) | copy-start | bytes 196612
  85.7 149.8 %all-reduce.5.cloned.1.call-start = ((), (), s32[]{:S(2)}) async-start(), calls=%async_computation.7 | async-start | bytes 524288 | tf_op jit(solution)/shard_map/psum | solution.py:67
  109.8 205.6 %copy-start.5 = (bf16[2,64]{1,0:T(2,128)(2,1)}, bf16[2,64]{1,0:T(2,128)(2,1)S(1)}, u32[]{:S(2)}) copy-start(bf16[2,64]{1,0:T(2,128)(2,1)S(1)} %copy.36) | copy-start | bytes 772
  159.0 188.9 %reduce-scatter.14.cloned.1.call-start = ((), (), s32[]{:S(2)}) async-start(), calls=%async_computation.11 | async-start | bytes 2359296
  313.4 35.6 %copy-start.4 = (bf16[2,512]{1,0:T(2,128)(2,1)S(1)}, bf16[2,512]{1,0:T(2,128)(2,1)}, u32[]{:S(2)}) copy-start(bf16[2,512]{1,0:T(2,128)(2,1)} %param.11) | copy-start | bytes 6148
  313.4 47.8 %copy-start.6 = (f32[512]{0:T(512)S(1)}, f32[512]{0:T(512)}, u32[]{:S(2)}) copy-start(f32[512]{0:T(512)} %param.19) | copy-start | bytes 6148
  315.5 175.3 %copy-start.1 = (bf16[192,512]{1,0:T(8,128)(2,1)S(1)}, bf16[192,512]{1,0:T(8,128)(2,1)}, u32[]{:S(2)}) copy-start(bf16[192,512]{1,0:T(8,128)(2,1)} %param.21) | copy-start | bytes 589828
  315.5 175.3 %all-reduce.7.cloned.1.call-start = ((), (), s32[]{:S(2)}) async-start(), calls=%async_computation.8 | async-start | bytes 393216 | tf_op jit(solution)/shard_map/psum | solution.py:102
  421.8 265.6 %all-reduce.9.cloned.1.call-start = ((), (), s32[]{:S(2)}) async-start(), calls=%async_computation.12 | async-start | bytes 524288
Sparse Core Ops, SparseCore 0:
  76.5 32.4 reduce-scatter.11
  111.8 45.0 reduce-scatter.9
  159.3 76.2 all-reduce.4
  315.6 32.3 reduce-scatter.13
  421.9 68.8 all-reduce.6
  494.1 193.2 all-reduce.8
